TPU v7x, 32 devices: a whole 2x2x4 slice. The times are simulated.
32 devices in a mesh: dp: 4 (over y, core), freq: 8 (over z, x).
Axes of the slice: x: 2, y: 2, z: 4, core: 2. Of those that a mesh axis runs over, the one named last changes fastest.
Arguments:
- grad_parts: float32 [4, 27, 4, 65536], P('dp', None, None, 'freq'), may hold values from -12 to 12
- kernel: float32 [27, 262144], P(None, ('dp', 'freq')), may hold values from -4 to 4
Outputs:
- clipped: float32 [27, 262144], P(None, ('dp', 'freq'))
All inputs are finite; a program needn't handle non-finite values.
Results may differ from a plain program's by a relative error of at most 0.0005.
The roundings to bfloat16 on the way count: a program that leaves them out, or rounds other values in their place, can miss the bound.
Values may be sent and summed in bfloat16 or wider, within the bound.
No kernel may reach another device: no remote copies, remote signals or barrier semaphores. Data moves between devices by JAX's collectives and lax.ppermute only.
A program may use at most 64 MiB of HBM per device.

v0:
```python
import math
import jax
import jax.numpy as jnp
from jax import lax
from jax.sharding import PartitionSpec as P

C = 512
TAPS = 27
GT = 8
GH = 32
GW = 32
KD = 2
CLIP = 0.25
HIGH = lax.Precision.HIGHEST


def tap_phases(freq_ids, stride):
    flat_index = freq_ids * stride
    freq_time = flat_index // (GH * GW)
    freq_row = flat_index // GW % GH
    freq_col = flat_index % GW
    taps = jnp.arange(TAPS, dtype=jnp.int32)
    off_time = taps // 9 - 1
    off_row = taps // 3 % 3 - 1
    off_col = taps % 3 - 1
    period = GT * GH * GW
    turns = (
        freq_time[:, None] * off_time[None, :] * (GH * GW)
        + freq_row[:, None] * off_row[None, :] * (GT * GW)
        + freq_col[:, None] * off_col[None, :] * (GT * GH)
    ) % period
    angle = turns.astype(jnp.float32) * (2.0 * math.pi / period)
    return (jnp.cos(angle), jnp.sin(angle))


def clip_factor(local_square):
    summed = lax.psum(local_square, ("dp", "freq"))
    return jnp.minimum(1.0, CLIP * math.sqrt(TAPS * C * C) / jnp.sqrt(summed + 1e-06))


def spectrum(field, cosine, sine_rows):
    real_spec = jnp.dot(cosine, field, precision=HIGH)
    imag_spec = -jnp.dot(sine_rows, field, precision=HIGH)
    return jnp.stack([real_spec, imag_spec], axis=1)


def taps_back(polar_part, cosine, sine_rows):
    values = polar_part.astype(jnp.float32)
    summed = jnp.dot(cosine.T, values[:, 0], precision=HIGH)
    return summed - jnp.dot(sine_rows.T, values[:, 1], precision=HIGH)


def polar_step(spectra):
    width = spectra.shape[-1]
    mean_square = jnp.mean(jnp.square(spectra.astype(jnp.float32)), axis=(1, 2, 3), keepdims=True)
    spread = math.sqrt(8.0 * width)
    scaled = (
        spectra.astype(jnp.float32) * (0.75 / (spread * jnp.sqrt(mean_square + 1e-06)))
    ).astype(jnp.bfloat16)
    real_part = scaled[:, 0]
    imag_part = scaled[:, 1]
    stacked = jnp.concatenate([real_part, imag_part], axis=1)
    turned = jnp.concatenate([imag_part, -real_part], axis=1)
    gram = jnp.einsum(
        "nri,nrj->nij",
        stacked,
        jnp.concatenate([stacked, turned], axis=2),
        preferred_element_type=jnp.float32,
    ).astype(jnp.bfloat16)
    gram_real = gram[:, :, :width]
    gram_imag = gram[:, :, width:]
    blocked = jnp.concatenate([gram, jnp.concatenate([-gram_imag, gram_real], axis=2)], axis=1)
    side = jnp.concatenate([real_part, imag_part], axis=2)
    product = jnp.einsum("nij,njk->nik", side, blocked, preferred_element_type=jnp.float32)
    result = (1.5 * side.astype(jnp.float32) - 0.5 * product).astype(jnp.bfloat16)
    return jnp.stack([result[:, :, :width], result[:, :, width:]], axis=1)


def on_device(grad_parts, kernel):
    devices_dp = lax.axis_size("dp")
    devices_freq = lax.axis_size("freq")
    total_freq = KD * devices_dp * devices_freq
    stride = GT * GH * GW // total_freq
    scale_out = math.sqrt(C / total_freq)
    own_width = kernel.shape[1]
    gradient = lax.psum_scatter(grad_parts[0], "dp", scatter_dimension=1, tiled=True).reshape(
        TAPS, own_width
    )
    local_square = jnp.sum(gradient * gradient)
    kernel_all, gradient_all = (kernel, gradient)
    freq_ids = jnp.arange(total_freq, dtype=jnp.int32)
    cosine, sine_rows = tap_phases(freq_ids, stride)
    factor = clip_factor(local_square)
    spectra = spectrum(kernel_all - factor * gradient_all, cosine, sine_rows)
    spectra = spectra.astype(jnp.bfloat16)
    count, row_width = (spectra.shape[0], spectra.shape[2])
    whole = lax.all_to_all(
        lax.all_to_all(
            spectra.reshape(count, 2, 1, 1, row_width),
            "dp",
            split_axis=0,
            concat_axis=2,
            tiled=True,
        ),
        "freq",
        split_axis=0,
        concat_axis=3,
        tiled=True,
    )
    polar_part = polar_step(whole.reshape(KD, 2, C, C))
    returned = lax.all_to_all(
        lax.all_to_all(
            polar_part.reshape(KD, 2, devices_dp, devices_freq, row_width),
            "dp",
            split_axis=2,
            concat_axis=0,
            tiled=True,
        ),
        "freq",
        split_axis=3,
        concat_axis=0,
        tiled=True,
    )
    position = jnp.arange(total_freq, dtype=jnp.int32)
    source_freq = position // (devices_dp * KD)
    source_dp = position // KD % devices_dp
    member = position % KD
    back_ids = source_dp * (devices_freq * KD) + source_freq * KD + member
    back_cos, back_sin = tap_phases(back_ids, stride)
    return taps_back(returned.reshape(count, 2, row_width), back_cos, back_sin) * scale_out


def solution(mesh):
    return jax.shard_map(
        on_device,
        mesh=mesh,
        in_specs=(P("dp", None, None, "freq"), P(None, ("dp", "freq"))),
        out_specs=P(None, ("dp", "freq")),
        check_vma=False,
    )
```

profile of v0, /device:TPU:0, one launch (start us, length us, event | category | flops | bytes accessed | tf_op | source)
XLA Modules:
  0.0 307.9 jit_solution(1594015570563499403)
XLA Ops:
  6.5 0.0 reduce-scatter.2.cloned.1.call-start
  6.5 6.0 %copy.47 = f32[1,27,4,8192]{3,1,2,0:T(8,128)} copy(f32[1,27,4,8192]{3,2,1,0:T(4,128)} %param.2) | data formatting | bytes 7077888 | tf_op args[0]
  12.5 0.0 copy-start.1
  12.5 0.0 reduce-scatter.2.cloned.1.call-update
  12.6 47.3 %reduce-scatter.2.cloned.1.call-done = f32[27,1,8192]{2,0,1:T(8,128)} async-done(((f32[27,4,8192]{2,0,1:T(8,128)}), f32[27,1,8192]{2,0,1:T(8,128)}) %reduce-scatter.2.cloned.1.call-update) | async-done | bytes 884752 | tf_op jit(solution)/shard_map/reduce_scatter | solution.py:86
  59.9 0.0 copy-start
  59.9 2.2 multiply_reduce_fusion.1
  62.1 39.5 %psum.7 = f32[]{:T(128)} all-reduce(f32[]{:T(128)} %multiply_reduce_fusion.1), channel_id=1, replica_groups=mesh['dp'=4,'freq'=8] {'dp','freq'}, use_global_device_ids=true, to_apply=%region_2.3 | all-reduce | flops 1 | bytes 8 | tf_op jit(solution)/shard_map/psum | solution.py:37
  102.3 0.0 copy-done.1
  102.3 3.2 %fusion.2 = bf16[64,1,1,1,8192]{4,0,3,2,1:T(8,128)(2,1)S(1)} fusion(f32[27,8192]{1,0:T(8,128)S(1)} %copy-done.1, f32[27,1,8192]{2,0,1:T(8,128)} %reduce-scatter.2.cloned.1.call-done, f32[]{:T(128)S(6)} %min_shard_map.3, s32[64]{0:T(128)S(1)} %get-tuple-element.11, s32[64]{0:T(128)S(1)} %get-tuple-element.12, s32[64]{0:T(128)S(1)} %and_select_fusion.3, ...), kind=kOutput, calls=%fused_computation.4 | convolution fusion | flops 171396544 | bytes 2819144 | tf_op jit(solution)/shard_map/dot_general | solution.py:43
  105.6 0.0 copy-done
  105.6 2.0 fusion.1
  107.6 0.2 pad_maximum_fusion
  107.8 2.2 copy.32
  110.0 29.2 %all_to_all.60 = bf16[64,2,1,1,8192]{4,1,3,2,0:T(2,128)(2,1)S(1)} all-to-all(bf16[64,2,1,1,8192]{4,1,3,2,0:T(2,128)(2,1)S(1)} %copy.32), channel_id=1, replica_groups=mesh['dp'=4,'freq'=8] {'dp'}, dimensions={0} | all-to-all | bytes 4194304 | tf_op jit(solution)/shard_map/all_to_all | solution.py:98
  139.2 1.2 copy.33
  140.4 1.6 copy.34
  142.0 52.3 %all_to_all.61 = bf16[16,2,4,1,8192]{4,2,1,3,0:T(4,128)(2,1)S(1)} all-to-all(bf16[16,2,4,1,8192]{4,2,1,3,0:T(4,128)(2,1)S(1)} %copy.34), channel_id=1, replica_groups=mesh['dp'=4,'freq'=8] {'freq'}, dimensions={0} | all-to-all | bytes 4194304 | tf_op jit(solution)/shard_map/all_to_all | solution.py:97
  194.3 1.2 multiply_reduce_fusion
  195.6 0.1 reduce_sum.27
  195.7 3.2 %copy.46 = f32[8,2,2,4,1,8192]{5,0,3,1,2,4:T(8,128)} copy(bf16[8,2,2,4,1,8192]{5,3,2,1,0,4:T(4,128)(2,1)S(1)} %bitcast.49) | data formatting | bytes 6291456 | tf_op jit(solution)/shard_map/convert_element_type | solution.py:58
  198.8 5.0 %reshape.259 = f32[2,2,512,512]{3,2,0,1:T(8,128)} reshape(f32[2,2,4,8,1,8192]{5,3,2,0,1,4:T(8,128)} %bitcast.50) | data formatting | bytes 8388608 | tf_op jit(solution)/shard_map/convert_element_type | solution.py:58
  203.8 2.8 multiply_convert_fusion
  206.6 0.1 fusion.83
  206.7 0.1 slice_bitcast_fusion.5
  206.9 2.6 fusion.23
  209.5 0.1 slice_negate_fusion
  209.6 2.6 subtract_convert_fusion
  212.2 0.2 fusion.84
  212.4 0.5 stack.21
  212.9 0.5 stack.22
  213.5 0.2 pad_maximum_fusion.2
  213.7 0.2 copy.42
  213.9 28.2 %all_to_all.62 = bf16[2,2,4,8,8192]{4,3,1,0,2:T(8,128)(2,1)S(1)} all-to-all(bf16[2,2,4,8,8192]{4,3,1,0,2:T(8,128)(2,1)S(1)} %copy.42), channel_id=1, replica_groups=mesh['dp'=4,'freq'=8] {'dp'}, dimensions={2} | all-to-all | bytes 4194304 | tf_op jit(solution)/shard_map/all_to_all | solution.py:112
  242.0 3.5 %copy.39 = bf16[8,2,1,8,8192]{4,1,0,2,3:T(2,128)(2,1)} copy(bf16[8,2,1,8,8192]{4,3,1,0,2:T(8,128)(2,1)S(1)} %bitcast.55) | data formatting | bytes 4194304 | tf_op jit(solution)/shard_map/all_to_all | solution.py:112
  245.6 3.6 %all-to-all-start.3 = ((bf16[8,2,1,8,8192]{4,1,0,2,3:T(2,128)(2,1)}), bf16[8,2,1,8,8192]{4,1,0,2,3:T(2,128)(2,1)S(1)}, u32[]{:S(2)}, u32[]{:S(2)}) async-start(bf16[8,2,1,8,8192]{4,1,0,2,3:T(2,128)(2,1)} %copy.39), calls=%async_computation.4 | async-start | bytes 4194304 | tf_op jit(solution)/shard_map/all_to_all | solution.py:111
  249.2 48.0 %all-to-all-done.3 = bf16[8,2,1,8,8192]{4,1,0,2,3:T(2,128)(2,1)S(1)} async-done(((bf16[8,2,1,8,8192]{4,1,0,2,3:T(2,128)(2,1)}), bf16[8,2,1,8,8192]{4,1,0,2,3:T(2,128)(2,1)S(1)}, u32[]{:S(2)}, u32[]{:S(2)}) %all-to-all-start.3) | async-done | bytes 2097184 | tf_op jit(solution)/shard_map/all_to_all | solution.py:111
  297.2 1.2 copy.48
  298.4 0.8 fusion.28
  299.2 1.8 fusion.3
  (8 shorter events, 0.1 us)
Async XLA Ops:
  6.5 53.4 %reduce-scatter.2.cloned.1.call-start = ((), (), s32[]{:S(2)}) async-start(), calls=%async_computation.5 | async-start | bytes 5242880 | tf_op jit(solution)/shard_map/reduce_scatter | solution.py:86
  12.5 89.8 %copy-start.1 = (f32[27,8192]{1,0:T(8,128)S(1)}, f32[27,8192]{1,0:T(8,128)}, u32[]{:S(2)}) copy-start(f32[27,8192]{1,0:T(8,128)} %param.3) | copy-start | bytes 2654212
  59.9 45.7 %copy-start = (f32[27,1,8192]{2,0,1:T(8,128)S(1)}, f32[27,1,8192]{2,0,1:T(8,128)}, u32[]{:S(2)}) copy-start(f32[27,1,8192]{2,0,1:T(8,128)} %reduce-scatter.2.cloned.1.call-done) | copy-start | bytes 2654212
  245.6 51.7 %all-to-all-start.3 = ((bf16[8,2,1,8,8192]{4,1,0,2,3:T(2,128)(2,1)}), bf16[8,2,1,8,8192]{4,1,0,2,3:T(2,128)(2,1)S(1)}, u32[]{:S(2)}, u32[]{:S(2)}) async-start(bf16[8,2,1,8,8192]{4,1,0,2,3:T(2,128)(2,1)} %copy.39), calls=%async_computation.4 | async-start | bytes 4194304 | tf_op jit(solution)/shard_map/all_to_all | solution.py:111
Sparse Core Ops, SparseCore 0:
  12.7 47.2 reduce-scatter.1
where the time goes:
time: 308 us
  blocking collectives  149 us (48%)
  waiting for transfers between devices  95.4 us (31%)
  local copies, waits for them, and re-layouts  25.4 us (8%)
  between operations  14.3 us (5%)
  matrix products  13 us (4%)
  other arithmetic  6.98 us (2%)
  starting transfers between devices  3.6 us (1%)
    all_to_all x1, blocking collectives, on_device(): lax.all_to_all(lax.all_to_all(spectra.reshape(count, 2, 1, 1, row_width),...  52.3 us
    all_to_all x1, waiting for transfers between devices, on_device(): lax.all_to_all(lax.all_to_all(polar_part.reshape(KD, 2, devices_dp, devic...  48 us
    reduce_scatter x1, waiting for transfers between devices, on_device(): lax.psum_scatter(grad_parts[0], 'dp', scatter_dimension=1, tiled=True)  47.3 us
    psum x1, blocking collectives, clip_factor(): summed = lax.psum(local_square, ('dp', 'freq'))  39.5 us
    all_to_all x1, blocking collectives, on_device(): lax.all_to_all(spectra.reshape(count, 2, 1, 1, row_width), 'dp', split_ax...  29.2 us
    all_to_all x1, blocking collectives, on_device(): lax.all_to_all(polar_part.reshape(KD, 2, devices_dp, devices_freq, row_wi...  28.2 us
    convert_element_type x2, local copies, waits for them, and re-layouts, polar_step(): spectra.astype(jnp.float32)  8.14 us
  transfers between devices with their start and end apart: 2, of which 2 were waited for; matrix products, arithmetic and copies ran while one was open for 0% of the time, Pallas kernels for 0%

commit v1 on v0

--- a/solution.py
+++ b/solution.py
@@ -3,6 +3,7 @@
 import jax.numpy as jnp
 from jax import lax
 from jax.sharding import PartitionSpec as P
+from jax.lax import psum
 
 C = 512
 TAPS = 27
@@ -34,7 +35,8 @@
 
 
 def clip_factor(local_square):
-    summed = lax.psum(local_square, ("dp", "freq"))
+    _attach_skins = lambda local_block: psum(psum(local_block, axis_name="freq"), axis_name="dp")
+    summed = _attach_skins(local_square)
     return jnp.minimum(1.0, CLIP * math.sqrt(TAPS * C * C) / jnp.sqrt(summed + 1e-06))
 
 

time: 308 us -> 295 us (0.958)
  blocking collectives: 149 us -> 135 us
    psum x1 -> x2, blocking collectives: 39.5 us -> 28.5 us  [the longest x1 22 us: clip_factor(): psum(local_block, axis_name='freq')]
where the time goes in v1:
time: 295 us; the launch traced here: 294 us
  blocking collectives  135 us (46%)
  waiting for transfers between devices  95.4 us (32%)
  local copies, waits for them, and re-layouts  25.4 us (9%)
  between operations  14.3 us (5%)
  matrix products  13 us (4%)
  other arithmetic  6.98 us (2%)
  starting transfers between devices  3.6 us (1%)
    all_to_all x1, blocking collectives, on_device(): lax.all_to_all(lax.all_to_all(spectra.reshape(count, 2, 1, 1, row_width),...  50.6 us
    all_to_all x1, waiting for transfers between devices, on_device(): lax.all_to_all(lax.all_to_all(polar_part.reshape(KD, 2, devices_dp, devic...  48 us
    reduce_scatter x1, waiting for transfers between devices, on_device(): lax.psum_scatter(grad_parts[0], 'dp', scatter_dimension=1, tiled=True)  47.3 us
    all_to_all x1, blocking collectives, on_device(): lax.all_to_all(spectra.reshape(count, 2, 1, 1, row_width), 'dp', split_ax...  28.2 us
    all_to_all x1, blocking collectives, on_device(): lax.all_to_all(polar_part.reshape(KD, 2, devices_dp, devices_freq, row_wi...  28.2 us
    psum x1, blocking collectives, clip_factor(): psum(local_block, axis_name='freq')  22 us
    convert_element_type x2, local copies, waits for them, and re-layouts, polar_step(): spectra.astype(jnp.float32)  8.14 us
    psum x1, blocking collectives, clip_factor(): psum(psum(local_block, axis_name='freq'), axis_name='dp')  6.59 us
  transfers between devices with their start and end apart: 2, of which 2 were waited for; matrix products, arithmetic and copies ran while one was open for 0% of the time, Pallas kernels for 0%

profile of v1, /device:TPU:0, one launch (start us, length us, event | category | flops | bytes accessed | tf_op | source)
XLA Modules:
  0.0 294.2 jit_solution(4403301753157289322)
XLA Ops:
  6.5 0.0 reduce-scatter.2.cloned.1.call-start
  6.5 6.0 %copy.47 = f32[1,27,4,8192]{3,1,2,0:T(8,128)} copy(f32[1,27,4,8192]{3,2,1,0:T(4,128)} %param.2) | data formatting | bytes 7077888 | tf_op args[0]
  12.5 0.0 copy-start.1
  12.5 0.0 reduce-scatter.2.cloned.1.call-update
  12.6 47.3 %reduce-scatter.2.cloned.1.call-done = f32[27,1,8192]{2,0,1:T(8,128)} async-done(((f32[27,4,8192]{2,0,1:T(8,128)}), f32[27,1,8192]{2,0,1:T(8,128)}) %reduce-scatter.2.cloned.1.call-update) | async-done | bytes 884752 | tf_op jit(solution)/shard_map/reduce_scatter | solution.py:88
  59.9 0.0 copy-start
  59.9 2.2 multiply_reduce_fusion.1
  62.1 22.0 %psum.14 = f32[]{:T(128)} all-reduce(f32[]{:T(128)} %multiply_reduce_fusion.1), channel_id=1, replica_groups=mesh['dp'=4,'freq'=8] {'freq'}, use_global_device_ids=true, to_apply=%region_2.3 | all-reduce | flops 1 | bytes 8 | tf_op jit(solution)/shard_map/psum | solution.py:38
  84.1 6.6 %psum.15 = f32[]{:T(128)} all-reduce(f32[]{:T(128)} %psum.14), channel_id=1, replica_groups=mesh['dp'=4,'freq'=8] {'dp'}, use_global_device_ids=true, to_apply=%region_3.4 | all-reduce | flops 1 | bytes 8 | tf_op jit(solution)/shard_map/psum | solution.py:38
  91.4 0.0 copy-done.1
  91.4 3.2 %fusion.2 = bf16[64,1,1,1,8192]{4,0,3,2,1:T(8,128)(2,1)S(1)} fusion(f32[27,8192]{1,0:T(8,128)S(1)} %copy-done.1, f32[27,1,8192]{2,0,1:T(8,128)} %reduce-scatter.2.cloned.1.call-done, f32[]{:T(128)S(6)} %min_shard_map.3, s32[64]{0:T(128)S(1)} %get-tuple-element.11, s32[64]{0:T(128)S(1)} %get-tuple-element.12, s32[64]{0:T(128)S(1)} %and_select_fusion.3, ...), kind=kOutput, calls=%fused_computation.4 | convolution fusion | flops 171396544 | bytes 2819144 | tf_op jit(solution)/shard_map/dot_general | solution.py:45
  94.6 0.0 copy-done
  94.6 2.0 fusion.1
  96.6 0.2 pad_maximum_fusion
  96.8 2.2 copy.32
  99.0 28.2 %all_to_all.60 = bf16[64,2,1,1,8192]{4,1,3,2,0:T(2,128)(2,1)S(1)} all-to-all(bf16[64,2,1,1,8192]{4,1,3,2,0:T(2,128)(2,1)S(1)} %copy.32), channel_id=1, replica_groups=mesh['dp'=4,'freq'=8] {'dp'}, dimensions={0} | all-to-all | bytes 4194304 | tf_op jit(solution)/shard_map/all_to_all | solution.py:100
  127.2 1.2 copy.33
  128.3 1.6 copy.34
  130.0 50.6 %all_to_all.61 = bf16[16,2,4,1,8192]{4,2,1,3,0:T(4,128)(2,1)S(1)} all-to-all(bf16[16,2,4,1,8192]{4,2,1,3,0:T(4,128)(2,1)S(1)} %copy.34), channel_id=1, replica_groups=mesh['dp'=4,'freq'=8] {'freq'}, dimensions={0} | all-to-all | bytes 4194304 | tf_op jit(solution)/shard_map/all_to_all | solution.py:99
  180.6 1.2 multiply_reduce_fusion
  181.8 0.1 reduce_sum.27
  181.9 3.2 %copy.46 = f32[8,2,2,4,1,8192]{5,0,3,1,2,4:T(8,128)} copy(bf16[8,2,2,4,1,8192]{5,3,2,1,0,4:T(4,128)(2,1)S(1)} %bitcast.49) | data formatting | bytes 6291456 | tf_op jit(solution)/shard_map/convert_element_type | solution.py:60
  185.1 5.0 %reshape.259 = f32[2,2,512,512]{3,2,0,1:T(8,128)} reshape(f32[2,2,4,8,1,8192]{5,3,2,0,1,4:T(8,128)} %bitcast.50) | data formatting | bytes 8388608 | tf_op jit(solution)/shard_map/convert_element_type | solution.py:60
  190.1 2.8 multiply_convert_fusion
  192.9 0.1 fusion.83
  193.0 0.1 slice_bitcast_fusion.5
  193.1 2.6 fusion.23
  195.7 0.1 slice_negate_fusion
  195.9 2.6 subtract_convert_fusion
  198.4 0.2 fusion.84
  198.6 0.5 stack.21
  199.2 0.5 stack.22
  199.7 0.2 pad_maximum_fusion.2
  199.9 0.2 copy.42
  200.1 28.2 %all_to_all.62 = bf16[2,2,4,8,8192]{4,3,1,0,2:T(8,128)(2,1)S(1)} all-to-all(bf16[2,2,4,8,8192]{4,3,1,0,2:T(8,128)(2,1)S(1)} %copy.42), channel_id=1, replica_groups=mesh['dp'=4,'freq'=8] {'dp'}, dimensions={2} | all-to-all | bytes 4194304 | tf_op jit(solution)/shard_map/all_to_all | solution.py:114
  228.3 3.5 %copy.39 = bf16[8,2,1,8,8192]{4,1,0,2,3:T(2,128)(2,1)} copy(bf16[8,2,1,8,8192]{4,3,1,0,2:T(8,128)(2,1)S(1)} %bitcast.55) | data formatting | bytes 4194304 | tf_op jit(solution)/shard_map/all_to_all | solution.py:114
  231.8 3.6 %all-to-all-start.3 = ((bf16[8,2,1,8,8192]{4,1,0,2,3:T(2,128)(2,1)}), bf16[8,2,1,8,8192]{4,1,0,2,3:T(2,128)(2,1)S(1)}, u32[]{:S(2)}, u32[]{:S(2)}) async-start(bf16[8,2,1,8,8192]{4,1,0,2,3:T(2,128)(2,1)} %copy.39), calls=%async_computation.4 | async-start | bytes 4194304 | tf_op jit(solution)/shard_map/all_to_all | solution.py:113
  235.5 48.0 %all-to-all-done.3 = bf16[8,2,1,8,8192]{4,1,0,2,3:T(2,128)(2,1)S(1)} async-done(((bf16[8,2,1,8,8192]{4,1,0,2,3:T(2,128)(2,1)}), bf16[8,2,1,8,8192]{4,1,0,2,3:T(2,128)(2,1)S(1)}, u32[]{:S(2)}, u32[]{:S(2)}) %all-to-all-start.3) | async-done | bytes 2097184 | tf_op jit(solution)/shard_map/all_to_all | solution.py:113
  283.5 1.2 copy.48
  284.7 0.8 fusion.28
  285.5 1.8 fusion.3
  (8 shorter events, 0.1 us)
Async XLA Ops:
  6.5 53.4 %reduce-scatter.2.cloned.1.call-start = ((), (), s32[]{:S(2)}) async-start(), calls=%async_computation.5 | async-start | bytes 5242880 | tf_op jit(solution)/shard_map/reduce_scatter | solution.py:88
  12.5 78.9 %copy-start.1 = (f32[27,8192]{1,0:T(8,128)S(1)}, f32[27,8192]{1,0:T(8,128)}, u32[]{:S(2)}) copy-start(f32[27,8192]{1,0:T(8,128)} %param.3) | copy-start | bytes 2654212
  59.9 34.7 %copy-start = (f32[27,1,8192]{2,0,1:T(8,128)S(1)}, f32[27,1,8192]{2,0,1:T(8,128)}, u32[]{:S(2)}) copy-start(f32[27,1,8192]{2,0,1:T(8,128)} %reduce-scatter.2.cloned.1.call-done) | copy-start | bytes 2654212
  231.8 51.7 %all-to-all-start.3 = ((bf16[8,2,1,8,8192]{4,1,0,2,3:T(2,128)(2,1)}), bf16[8,2,1,8,8192]{4,1,0,2,3:T(2,128)(2,1)S(1)}, u32[]{:S(2)}, u32[]{:S(2)}) async-start(bf16[8,2,1,8,8192]{4,1,0,2,3:T(2,128)(2,1)} %copy.39), calls=%async_computation.4 | async-start | bytes 4194304 | tf_op jit(solution)/shard_map/all_to_all | solution.py:113
Sparse Core Ops, SparseCore 0:
  12.7 47.2 reduce-scatter.1
